TPU v7x, 256 devices: a whole 4x4x8 slice. The times are simulated.
256 devices in a mesh: dp: 32 (over x, y, core), tensor: 8 (over z).
Axes of the slice: x: 4, y: 4, z: 8, core: 2. Of those that a mesh axis runs over, the one named last changes fastest.
Arguments:
- hidden_states: bfloat16 [24576, 4096], P('dp', 'tensor')
- neighbour_ids: int32 [384, 2], P('dp'), may hold values from 0 to 511, as said below
- database: bfloat16 [512, 128, 896], P('dp')
- w_up: bfloat16 [896, 3584], P(None, 'tensor'), may hold values from -0.1875 to 0.1875
- w_down: bfloat16 [3584, 896], P('tensor'), may hold values from -0.09375 to 0.09375
- w_query: bfloat16 [4096, 4096], P(None, 'tensor'), may hold values from -0.09375 to 0.09375
- w_key: bfloat16 [896, 4096], P(None, 'tensor'), may hold values from -0.1875 to 0.1875
- w_value: bfloat16 [896, 4096], P(None, 'tensor'), may hold values from -0.1875 to 0.1875
Outputs:
- attended: bfloat16 [24576, 4096], P('dp', 'tensor')
Inputs may be any that keep to these rules, and one draw needn't show every extreme that they name: `neighbour_ids`: block ids are grouped by owner: index s of dp holds blocks s * 16 to (s + 1) * 16 - 1. Among the 24 ids of one sequence, no owner's blocks are named more than 2 times; one owner, the same for every sequence, is named exactly 2 times by each.
All inputs are finite; a program needn't handle non-finite values.
Results may differ from a plain program's by a relative error of at most 0.02.
Values may be sent and summed in bfloat16 or wider, within the bound.
No kernel may reach another device: no remote copies, remote signals or barrier semaphores. Data moves between devices by JAX's collectives and lax.ppermute only.
A program may use at most 128 MiB of HBM per device.

v0:
```python
import math
import jax
import jax.numpy as jnp
from jax import lax
from jax.sharding import PartitionSpec as P

HD = 128
SPAN = 64
KN = 2
NTOK = 128
EPSILON = 1e-06
LOGIT_SCALE = 3.0


def head_norm(projected):
    shaped = projected.reshape(projected.shape[0], -1, HD)
    scaled = shaped * lax.rsqrt(jnp.mean(shaped * shaped, axis=-1, keepdims=True) + EPSILON)
    return scaled.astype(jnp.bfloat16)


def attend(windows_flat, keys, values):
    heads_here = windows_flat.shape[1]
    span_count = windows_flat.shape[0] // SPAN
    windows = windows_flat.reshape(span_count, SPAN, heads_here, HD)
    key_blocks = keys.reshape(span_count, KN * NTOK, heads_here, HD)
    value_blocks = values.reshape(span_count, KN * NTOK, heads_here, HD)
    scores = jnp.einsum("cqhd,ckhd->chqk", windows, key_blocks, preferred_element_type=jnp.float32)
    scores = scores * (LOGIT_SCALE / math.sqrt(HD))
    expo = jnp.exp(scores)
    weights = (expo / jnp.sum(expo, axis=-1, keepdims=True)).astype(jnp.bfloat16)
    mixed = jnp.einsum("chqk,ckhd->cqhd", weights, value_blocks, preferred_element_type=jnp.float32)
    return mixed.astype(jnp.bfloat16).reshape(span_count * SPAN, heads_here * HD)


def ring_hops(states, n):
    to_right = [(i, (i + 1) % n) for i in range(n)]
    to_left = [(i, (i - 1) % n) for i in range(n)]
    going_right = states
    going_left = states
    right_hops = n // 2
    left_hops = n - 1 - right_hops
    steps = []
    for hop in range(1, right_hops + 1):
        step = {}
        going_right = lax.ppermute(going_right, "tensor", to_right)
        step[(n - hop) % n] = going_right
        if hop <= left_hops:
            going_left = lax.ppermute(going_left, "tensor", to_left)
            step[hop] = going_left
        steps.append(step)
    return steps


def ring_query(got, w_query, n):
    width = got[0].shape[1]
    me = lax.axis_index("tensor")
    total = None
    for offset in range(n):
        rows = lax.dynamic_slice_in_dim(w_query, (me + offset) % n * width, width, 0)
        term = jnp.dot(got[offset], rows, preferred_element_type=jnp.float32)
        total = term if total is None else total + term
    return total


def shards(hidden_states, neighbour_ids, database, w_up, w_down, w_query, w_key, w_value):
    dp_count = lax.axis_size("dp")
    tensor_count = lax.axis_size("tensor")
    shard_blocks = database.shape[0]
    block_tokens = database.shape[1]
    enc_width = database.shape[2]
    flat_ids = neighbour_ids.reshape(-1)
    request_count = flat_ids.shape[0]
    capacity = max(2, (request_count + dp_count - 1) // dp_count + 1)
    owners = flat_ids // shard_blocks
    local_rows = flat_ids % shard_blocks
    owner_match = (owners[:, None] == jnp.arange(dp_count, dtype=jnp.int32)[None, :]).astype(
        jnp.int32
    )
    positions = jnp.arange(request_count, dtype=jnp.int32)
    earlier = (positions[:, None] > positions[None, :]).astype(jnp.int32)
    ranks = jnp.sum(jnp.dot(earlier, owner_match) * owner_match, axis=1)
    slots = owners * capacity + ranks
    slot_match = slots[None, :] == jnp.arange(dp_count * capacity, dtype=jnp.int32)[:, None]
    requests = jnp.sum(jnp.where(slot_match, local_rows[None, :], 0), axis=1)
    requests = requests.reshape(dp_count, capacity)
    pieces = dp_count
    me_dp = lax.axis_index("dp")
    up_piece = lax.dynamic_slice_in_dim(
        w_up, me_dp * (w_up.shape[0] // pieces), w_up.shape[0] // pieces, 0
    )
    down_piece = lax.dynamic_slice_in_dim(
        w_down, me_dp * (w_down.shape[0] // pieces), w_down.shape[0] // pieces, 0
    )
    up_all = lax.all_gather(lax.all_gather(up_piece, "tensor"), "dp")
    down_all = lax.all_gather(lax.all_gather(down_piece, "tensor"), "dp")
    rows_here = block_tokens // tensor_count
    raw_float = database.astype(jnp.float32)
    raw_own = lax.dynamic_slice_in_dim(
        raw_float, lax.axis_index("tensor") * rows_here, rows_here, 1
    )
    normed = (
        raw_own * lax.rsqrt(jnp.mean(raw_own * raw_own, axis=-1, keepdims=True) + EPSILON)
    ).astype(jnp.bfloat16)
    states = hidden_states[SPAN - 1 :]
    steps = ring_hops(states, tensor_count)
    got = {0: states}
    for step in steps:
        got.update(step)
    early = [v for step in steps[: len(steps) // 2] for v in step.values()]
    late = [v for step in steps[len(steps) // 2 :] for v in step.values()]
    normed, _ = lax.optimization_barrier((normed, early))
    flat_normed = normed.reshape(shard_blocks * rows_here, pieces, enc_width // pieces)
    inner = jnp.einsum("ncr,cgrh->ngh", flat_normed, up_all, preferred_element_type=jnp.float32)
    active = jax.nn.gelu(inner).astype(jnp.bfloat16)
    active = active.reshape(active.shape[0], tensor_count, pieces, -1)
    partials = jnp.einsum("ngcr,cgre->gne", active, down_all, preferred_element_type=jnp.float32)
    summed = jnp.sum(partials.astype(jnp.bfloat16).astype(jnp.float32), axis=0)
    summed = summed.reshape(shard_blocks, rows_here, enc_width)
    encoded_own = (raw_own + summed).astype(jnp.bfloat16)
    asked = lax.all_to_all(requests, "dp", split_axis=0, concat_axis=0, tiled=True)
    served, _ = lax.optimization_barrier((encoded_own[asked], late))
    replies = lax.all_to_all(served, "dp", split_axis=0, concat_axis=0, tiled=True)
    mine = replies.reshape(dp_count * capacity, rows_here, enc_width)[slots]
    queries = head_norm(ring_query(got, w_query, tensor_count))
    padded = jnp.concatenate(
        [queries, jnp.zeros((SPAN - 1,) + queries.shape[1:], queries.dtype)], axis=0
    )
    encoded = lax.all_gather(mine, "tensor", axis=1, tiled=True)
    flat_encoded = encoded.reshape(-1, enc_width)
    keys = head_norm(jnp.dot(flat_encoded, w_key, preferred_element_type=jnp.float32))
    values = jnp.dot(flat_encoded, w_value, preferred_element_type=jnp.float32).astype(jnp.bfloat16)
    values = values.reshape(flat_encoded.shape[0], -1, HD)
    mixed = [attend(padded, keys, values)]
    mixed = jnp.concatenate(mixed, axis=0)
    heads_width = mixed.shape[1]
    leading = jnp.zeros((SPAN - 1, heads_width), jnp.bfloat16)
    return jnp.concatenate([leading, mixed[: mixed.shape[0] - SPAN + 1]], axis=0)


def solution(mesh):
    in_specs = (
        P("dp", "tensor"),
        P("dp", None),
        P("dp", None, None),
        P(None, "tensor"),
        P("tensor", None),
        P(None, "tensor"),
        P(None, "tensor"),
        P(None, "tensor"),
    )
    out_specs = P("dp", "tensor")
    return jax.shard_map(shards, mesh=mesh, in_specs=in_specs, out_specs=out_specs, check_vma=False)
```

profile of v0, /device:TPU:1, one launch (start us, length us, event | category | flops | bytes accessed | tf_op | source)
XLA Modules:
  0.0 297.0 jit_solution(3649769576130073630)
XLA Ops:
  6.5 1.1 constant_dynamic-slice_fusion
  7.8 23.3 %all-gather.5 = bf16[8,28,448]{2,1,0:T(8,128)(2,1)S(1)} all-gather(bf16[1,28,448]{2,1,0:T(8,128)(2,1)S(1)} %bitcast.67), channel_id=2, replica_groups=mesh['dp'=32,'tensor'=8] {'tensor'}, dimensions={0}, use_global_device_ids=true | all-gather | bytes 225792 | tf_op jit(solution)/shard_map/all_gather | solution.py:94
  31.1 0.8 copy.93
  32.0 0.8 dynamic-slice_bitcast_fusion
  32.8 18.7 %all-gather.6 = bf16[8,14,896]{2,1,0:T(8,128)(2,1)S(1)} all-gather(bf16[1,14,896]{2,1,0:T(8,128)(2,1)S(1)} %dynamic-slice_bitcast_fusion), channel_id=4, replica_groups=mesh['dp'=32,'tensor'=8] {'tensor'}, dimensions={0}, use_global_device_ids=true | all-gather | bytes 225792 | tf_op jit(solution)/shard_map/all_gather | solution.py:95
  51.5 0.7 copy.97
  52.2 1.3 slice.6
  53.5 0.7 collective-permute-start
  54.2 2.1 collective-permute-start.1
  56.3 9.1 %collective-permute-done = bf16[705,512]{1,0:T(8,128)(2,1)S(1)} collective-permute-done((bf16[705,512]{1,0:T(8,128)(2,1)S(1)}, bf16[705,512]{1,0:T(8,128)(2,1)S(1)}, u32[]{:S(2)}, u32[]{:S(2)}) %collective-permute-start) | collective-permute-done | bytes 721952 | tf_op jit(solution)/shard_map/ppermute | solution.py:45
  66.0 0.7 all_to_all.11
  66.7 27.0 %all-to-all-start = ((s32[32,1,2]{2,1,0:T(1,128)}), s32[32,1,2]{2,1,0:T(1,128)S(1)}, u32[]{:S(2)}, u32[]{:S(2)}) async-start(s32[32,1,2]{2,1,0:T(1,128)} %bitcast.11), calls=%async_computation | async-start | bytes 32768 | tf_op jit(solution)/shard_map/all_to_all | solution.py:120
  93.8 1.2 fusion.37
  95.0 3.0 %collective-permute-start.3 = (bf16[705,512]{1,0:T(8,128)(2,1)S(1)}, bf16[705,512]{1,0:T(8,128)(2,1)}, u32[]{:S(2)}, u32[]{:S(2)}) collective-permute-start(bf16[705,512]{1,0:T(8,128)(2,1)S(1)} %collective-permute-done.1), channel_id=1, source_target_pairs={{0,7},{1,0},{2,1},{3,2},{4,3},{5,4},{6,5},{7,6},{8,15},{9,8},{10,9... | collective-permute-start | bytes 2165768 | tf_op jit(solution)/shard_map/ppermute | solution.py:48
  98.0 1.2 fusion.38
  99.2 1.5 all-to-all-done
  101.0 12.4 %collective-permute-done.3 = bf16[705,512]{1,0:T(8,128)(2,1)} collective-permute-done((bf16[705,512]{1,0:T(8,128)(2,1)S(1)}, bf16[705,512]{1,0:T(8,128)(2,1)}, u32[]{:S(2)}, u32[]{:S(2)}) %collective-permute-start.3) | collective-permute-done | bytes 721952 | tf_op jit(solution)/shard_map/ppermute | solution.py:48
  113.4 5.3 %reshape.242 = bf16[256,32,28]{2,1,0:T(8,128)(2,1)S(1)} reshape(bf16[16,16,896]{2,1,0:T(8,128)(2,1)S(1)} %fusion.38) | data formatting | bytes 917504 | tf_op jit(solution)/shard_map/reshape | solution.py:112
  118.8 3.0 %copy.94 = bf16[256,32,28]{0,1,2:T(8,128)(2,1)} copy(bf16[256,32,28]{2,1,0:T(8,128)(2,1)S(1)} %reshape.242) | data formatting | bytes 917504 | tf_op jit(solution)/shard_map/reshape | solution.py:112
  121.8 3.5 %collective-permute-start.5 = (bf16[705,512]{1,0:T(8,128)(2,1)}, bf16[705,512]{1,0:T(8,128)(2,1)}, u32[]{:S(2)}, u32[]{:S(2)}) collective-permute-start(bf16[705,512]{1,0:T(8,128)(2,1)} %collective-permute-done.3), channel_id=1, source_target_pairs={{0,7},{1,0},{2,1},{3,2},{4,3},{5,4},{6,5},{7,6},{8,15},{9,8},{10,9... | collective-permute-start | bytes 2165768 | tf_op jit(solution)/shard_map/ppermute | solution.py:48
  125.3 8.6 %fusion.11 = bf16[256,8,448]{0,2,1:T(8,128)(2,1)S(1)} fusion(bf16[32,8,28,448]{3,1,0,2:T(8,128)(2,1)} %bitcast.68, bf16[256,32,28]{0,1,2:T(8,128)(2,1)} %copy.94), kind=kOutput, calls=%fused_computation.19 | convolution fusion | flops 1652424704 | bytes 8716288 | tf_op jit(solution)/shard_map/ncr,cgrh->ngh/dot_general | solution.py:113
  133.9 1.0 copy.96
  134.9 20.9 %all-gather.13.cloned.1.call-done = bf16[256,14,896]{2,0,1:T(8,128)(2,1)} async-done(((bf16[8,14,896]{2,0,1:T(8,128)(2,1)}), bf16[256,14,896]{2,0,1:T(8,128)(2,1)}) %all-gather.13.cloned.1.call-update) | async-done | bytes 6422544 | tf_op jit(solution)/shard_map/all_gather | solution.py:95
  155.8 6.7 %convert_reduce_fusion = f32[256,896]{1,0:T(8,128)S(1)} fusion(bf16[32,8,14,896]{3,1,0,2:T(8,128)(2,1)} %bitcast.69, bf16[256,8,32,14]{0,1,3,2:T(8,128)(2,1)S(1)} %bitcast.63), kind=kOutput, calls=%fused_computation.5 | convolution fusion | flops 1649442816 | bytes 9175040 | tf_op jit(solution)/shard_map/ngcr,cgre->gne/dot_general | solution.py:116
  162.5 1.1 fusion.36
  163.6 2.0 gather_fusion
  165.6 4.7 %all-to-all-start.1 = ((bf16[32,2,16,896]{3,2,1,0:T(8,128)(2,1)}), bf16[32,2,16,896]{3,2,1,0:T(8,128)(2,1)S(1)}, u32[]{:S(2)}, u32[]{:S(2)}) async-start(bf16[32,2,16,896]{3,2,1,0:T(8,128)(2,1)} %bitcast.13), calls=%async_computation.1 | async-start | bytes 3670016 | tf_op jit(solution)/shard_map/all_to_all | solution.py:122
  170.7 25.1 %all-to-all-done.1 = bf16[32,2,16,896]{3,2,1,0:T(8,128)(2,1)S(1)} async-done(((bf16[32,2,16,896]{3,2,1,0:T(8,128)(2,1)}), bf16[32,2,16,896]{3,2,1,0:T(8,128)(2,1)S(1)}, u32[]{:S(2)}, u32[]{:S(2)}) %all-to-all-start.1) | async-done | bytes 1835040 | tf_op jit(solution)/shard_map/all_to_all | solution.py:122
  195.8 1.5 gather_fusion.1
  197.5 2.3 copy.114
  199.8 2.0 fusion.50
  201.8 0.6 copy-done.1
  203.5 1.7 fusion.42
  205.2 1.7 convolution_add_fusion.2
  206.8 1.7 fusion.44
  208.5 1.7 convolution_add_fusion.1
  210.2 1.8 fusion.27
  211.9 1.8 reshape.249
  213.7 0.8 multiply_reduce_fusion.1
  215.2 46.8 %all-gather.15.cloned.1.call-done = bf16[24,128,896]{2,1,0:T(8,128)(2,1)} async-done(((bf16[24,16,896]{2,1,0:T(8,128)(2,1)}), bf16[24,128,896]{2,1,0:T(8,128)(2,1)}) %all-gather.15.cloned.1.call-update) | async-done | bytes 5505040 | tf_op jit(solution)/shard_map/all_gather | solution.py:128
  262.0 8.7 %multiply_reduce_fusion = (f32[3072,4]{0,1:T(4,128)S(1)}, f32[3072,4,128]{2,0,1:T(8,128)}) fusion(bf16[3072,896,1]{1,0,2:T(8,128)(2,1)} %bitcast.70, bf16[4,128,896]{2,1,0:T(8,128)(2,1)S(1)} %bitcast.65), kind=kOutput, calls=%fused_computation.9 | convolution fusion | flops 2821705728 | bytes 12763136 | tf_op jit(solution)/shard_map/dot_general | solution.py:130
  270.8 4.8 %convolution_convert_fusion = bf16[3072,512]{1,0:T(8,128)(2,1)} fusion(bf16[3072,896]{1,0:T(8,128)(2,1)S(1)} %bitcast.71, bf16[896,512]{1,0:T(8,128)(2,1)S(1)} %copy-done), kind=kOutput, calls=%fused_computation.11 | convolution fusion | flops 2820145152 | bytes 9568256 | tf_op jit(solution)/shard_map/dot_general | solution.py:131
  275.5 5.5 %reshape_reshape.3 = bf16[12,256,4,128]{3,2,1,0:T(4,128)(2,1)} reshape(bf16[3072,512]{1,0:T(8,128)(2,1)} %convolution_convert_fusion) | data formatting | bytes 6291456 | tf_op jit(solution)/shard_map/reshape;reshape | solution.py:26
  281.1 4.4 %multiply_convert_fusion = bf16[3072,4,128]{2,0,1:T(8,128)(2,1)S(1)} fusion(f32[3072,4,128]{2,0,1:T(8,128)} %get-tuple-element.12, f32[3072,4]{0,1:T(4,128)S(1)} %add_rsqrt_fusion), kind=kLoop, calls=%fused_computation.8 | loop fusion | flops 3145728 | bytes 9486336 | tf_op jit(solution)/shard_map/convert_element_type | solution.py:18
  285.5 1.3 fusion.16
  287.4 1.2 fusion.32
  288.6 0.6 copy.111
  289.4 1.1 concatenate.7
  (59 shorter events, 4.1 us)
Async XLA Ops:
  6.5 264.2 %copy-start = (bf16[896,512]{1,0:T(8,128)(2,1)S(1)}, bf16[896,512]{1,0:T(8,128)(2,1)}, u32[]{:S(2)}) copy-start(bf16[896,512]{1,0:T(8,128)(2,1)} %param.15) | copy-start | bytes 2752516
  6.5 58.9 %copy-start.8 = (s32[12,2]{0,1:T(2,128)S(1)}, s32[12,2]{0,1:T(2,128)}, u32[]{:S(2)}) copy-start(s32[12,2]{0,1:T(2,128)} %param.9) | copy-start | bytes 292
  6.5 118.8 %all-gather.11.cloned.1.call-start = ((), (), s32[]{:S(2)}) async-start(), calls=%async_computation.2 | async-start | bytes 7569408 | tf_op jit(solution)/shard_map/all_gather | solution.py:94
  31.9 123.9 %all-gather.13.cloned.1.call-start = ((), (), s32[]{:S(2)}) async-start(), calls=%async_computation.3 | async-start | bytes 6623232 | tf_op jit(solution)/shard_map/all_gather | solution.py:95
  53.5 11.9 %collective-permute-start = (bf16[705,512]{1,0:T(8,128)(2,1)S(1)}, bf16[705,512]{1,0:T(8,128)(2,1)S(1)}, u32[]{:S(2)}, u32[]{:S(2)}) collective-permute-start(bf16[705,512]{1,0:T(8,128)(2,1)S(1)} %slice.6), channel_id=1, source_target_pairs={{0,1},{1,2},{2,3},{3,4},{4,5},{5,6},{6,7},{7,0},{8,9},{9,10},{10,1... | collective-permute-start | bytes 2165768 | tf_op jit(solution)/shard_map/ppermute | solution.py:45
  54.2 40.8 %collective-permute-start.1 = (bf16[705,512]{1,0:T(8,128)(2,1)S(1)}, bf16[705,512]{1,0:T(8,128)(2,1)S(1)}, u32[]{:S(2)}, u32[]{:S(2)}) collective-permute-start(bf16[705,512]{1,0:T(8,128)(2,1)S(1)} %slice.6), channel_id=1, source_target_pairs={{0,7},{1,0},{2,1},{3,2},{4,3},{5,4},{6,5},{7,6},{8,15},{9,8},{10,9... | collective-permute-start | bytes 2165768 | tf_op jit(solution)/shard_map/ppermute | solution.py:48
  65.4 35.6 %copy-start.4 = (bf16[705,512]{1,0:T(8,128)(2,1)}, bf16[705,512]{1,0:T(8,128)(2,1)S(1)}, u32[]{:S(2)}) copy-start(bf16[705,512]{1,0:T(8,128)(2,1)S(1)} %collective-permute-done) | copy-start | bytes 2165764
  65.4 32.6 %collective-permute-start.2 = (bf16[705,512]{1,0:T(8,128)(2,1)S(1)}, bf16[705,512]{1,0:T(8,128)(2,1)}, u32[]{:S(2)}, u32[]{:S(2)}) collective-permute-start(bf16[705,512]{1,0:T(8,128)(2,1)S(1)} %collective-permute-done), channel_id=1, source_target_pairs={{0,1},{1,2},{2,3},{3,4},{4,5},{5,6},{6,7},{7,0},{8,9},{9,10},{10,1... | collective-permute-start | bytes 2165768 | tf_op jit(solution)/shard_map/ppermute | solution.py:45
  66.7 34.0 %all-to-all-start = ((s32[32,1,2]{2,1,0:T(1,128)}), s32[32,1,2]{2,1,0:T(1,128)S(1)}, u32[]{:S(2)}, u32[]{:S(2)}) async-start(s32[32,1,2]{2,1,0:T(1,128)} %bitcast.11), calls=%async_computation | async-start | bytes 32768 | tf_op jit(solution)/shard_map/all_to_all | solution.py:120
  95.0 6.1 %copy-start.6 = (bf16[705,512]{1,0:T(8,128)(2,1)}, bf16[705,512]{1,0:T(8,128)(2,1)S(1)}, u32[]{:S(2)}) copy-start(bf16[705,512]{1,0:T(8,128)(2,1)S(1)} %collective-permute-done.1) | copy-start | bytes 2165764
  95.0 18.5 %collective-permute-start.3 = (bf16[705,512]{1,0:T(8,128)(2,1)S(1)}, bf16[705,512]{1,0:T(8,128)(2,1)}, u32[]{:S(2)}, u32[]{:S(2)}) collective-permute-start(bf16[705,512]{1,0:T(8,128)(2,1)S(1)} %collective-permute-done.1), channel_id=1, source_target_pairs={{0,7},{1,0},{2,1},{3,2},{4,3},{5,4},{6,5},{7,6},{8,15},{9,8},{10,9... | collective-permute-start | bytes 2165768 | tf_op jit(solution)/shard_map/ppermute | solution.py:48
  98.0 27.3 %collective-permute-start.4 = (bf16[705,512]{1,0:T(8,128)(2,1)}, bf16[705,512]{1,0:T(8,128)(2,1)}, u32[]{:S(2)}, u32[]{:S(2)}) collective-permute-start(bf16[705,512]{1,0:T(8,128)(2,1)} %collective-permute-done.2), channel_id=1, source_target_pairs={{0,1},{1,2},{2,3},{3,4},{4,5},{5,6},{6,7},{7,0},{8,9},{9,10},{10,1... | collective-permute-start | bytes 2165768 | tf_op jit(solution)/shard_map/ppermute | solution.py:45
  121.8 43.9 %collective-permute-start.5 = (bf16[705,512]{1,0:T(8,128)(2,1)}, bf16[705,512]{1,0:T(8,128)(2,1)}, u32[]{:S(2)}, u32[]{:S(2)}) collective-permute-start(bf16[705,512]{1,0:T(8,128)(2,1)} %collective-permute-done.3), channel_id=1, source_target_pairs={{0,7},{1,0},{2,1},{3,2},{4,3},{5,4},{6,5},{7,6},{8,15},{9,8},{10,9... | collective-permute-start | bytes 2165768 | tf_op jit(solution)/shard_map/ppermute | solution.py:48
  125.3 40.3 %collective-permute-start.6 = (bf16[705,512]{1,0:T(8,128)(2,1)}, bf16[705,512]{1,0:T(8,128)(2,1)S(1)}, u32[]{:S(2)}, u32[]{:S(2)}) collective-permute-start(bf16[705,512]{1,0:T(8,128)(2,1)} %collective-permute-done.4), channel_id=1, source_target_pairs={{0,1},{1,2},{2,3},{3,4},{4,5},{5,6},{6,7},{7,0},{8,9},{9,10},{10,1... | collective-permute-start | bytes 2165768 | tf_op jit(solution)/shard_map/ppermute | solution.py:45
  165.6 30.2 %all-to-all-start.1 = ((bf16[32,2,16,896]{3,2,1,0:T(8,128)(2,1)}), bf16[32,2,16,896]{3,2,1,0:T(8,128)(2,1)S(1)}, u32[]{:S(2)}, u32[]{:S(2)}) async-start(bf16[32,2,16,896]{3,2,1,0:T(8,128)(2,1)} %bitcast.13), calls=%async_computation.1 | async-start | bytes 3670016 | tf_op jit(solution)/shard_map/all_to_all | solution.py:122
  170.3 91.7 %all-gather.15.cloned.1.call-start = ((), (), s32[]{:S(2)}) async-start(), calls=%async_computation.4 | async-start | bytes 6193152 | tf_op jit(solution)/shard_map/all_gather | solution.py:128
  197.5 4.3 %copy-start.5 = (bf16[705,512]{1,0:T(8,128)(2,1)S(1)}, bf16[705,512]{1,0:T(8,128)(2,1)}, u32[]{:S(2)}) copy-start(bf16[705,512]{1,0:T(8,128)(2,1)} %copy-done.4) | copy-start | bytes 2165764
  199.8 2.6 copy-start.1
  199.8 3.1 %copy-start.7 = (bf16[705,512]{1,0:T(8,128)(2,1)S(1)}, bf16[705,512]{1,0:T(8,128)(2,1)}, u32[]{:S(2)}) copy-start(bf16[705,512]{1,0:T(8,128)(2,1)} %copy-done.6) | copy-start | bytes 2165764
  214.6 47.4 %copy-start.3 = (bf16[512,896]{1,0:T(8,128)(2,1)S(1)}, bf16[512,896]{1,0:T(8,128)(2,1)}, u32[]{:S(2)}) copy-start(bf16[512,896]{1,0:T(8,128)(2,1)} %copy.114) | copy-start | bytes 2752516
  262.0 8.7 %copy-start.9 = (bf16[24,128,896]{2,1,0:T(8,128)(2,1)S(1)}, bf16[24,128,896]{2,1,0:T(8,128)(2,1)}, u32[]{:S(2)}) copy-start(bf16[24,128,896]{2,1,0:T(8,128)(2,1)} %all-gather.15.cloned.1.call-done) | copy-start | bytes 16515076
  285.5 1.9 copy-start.2
Sparse Core Ops, SparseCore 0:
  32.0 66.9 all-gather.10
  101.6 54.1 all-gather.12
  197.5 64.4 all-gather.14
where the time goes:
time: 298 us; the launch traced here: 297 us
  waiting for transfers between devices  116 us (39%)
  matrix products  43 us (14%)
  blocking collectives  42 us (14%)
  starting transfers between devices  41.3 us (14%)
  local copies, waits for them, and re-layouts  31.8 us (11%)
  between operations  13.6 us (5%)
  other arithmetic  9.35 us (3%)
    all_gather x1, waiting for transfers between devices, shards(): encoded = lax.all_gather(mine, 'tensor', axis=1, tiled=True)  46.8 us
    all_to_all x1, starting transfers between devices, shards(): lax.all_to_all(requests, 'dp', split_axis=0, concat_axis=0, tiled=True)  27 us
    all_to_all x1, waiting for transfers between devices, shards(): lax.all_to_all(served, 'dp', split_axis=0, concat_axis=0, tiled=True)  25.1 us
    all_gather x1, blocking collectives, shards(): up_all = lax.all_gather(lax.all_gather(up_piece, 'tensor'), 'dp')  23.3 us
    all_gather x1, waiting for transfers between devices, shards(): down_all = lax.all_gather(lax.all_gather(down_piece, 'tensor'), 'dp')  20.9 us
    all_gather x1, blocking collectives, shards(): down_all = lax.all_gather(lax.all_gather(down_piece, 'tensor'), 'dp')  18.7 us
    ppermute x3, waiting for transfers between devices, ring_hops(): going_left = lax.ppermute(going_left, 'tensor', to_left)  12.4 us
    dot_general x8, matrix products, ring_query(): term = jnp.dot(got[offset], rows, preferred_element_type=jnp.float32)  11.5 us
  transfers between devices with their start and end apart: 12, of which 6 were waited for; matrix products, arithmetic and copies ran while one was open for 17% of the time, Pallas kernels for 0%

commit v1 on v0

--- a/solution.py
+++ b/solution.py
@@ -125,7 +125,10 @@
     padded = jnp.concatenate(
         [queries, jnp.zeros((SPAN - 1,) + queries.shape[1:], queries.dtype)], axis=0
     )
-    encoded = lax.all_gather(mine, "tensor", axis=1, tiled=True)
+    local_now = lax.axis_size("tensor")
+    passed = jnp.stack(local_now * [mine], axis=0)
+    formed = lax.all_to_all(passed, "tensor", 0, 0)
+    encoded = jnp.concatenate(formed, axis=1)
     flat_encoded = encoded.reshape(-1, enc_width)
     keys = head_norm(jnp.dot(flat_encoded, w_key, preferred_element_type=jnp.float32))
     values = jnp.dot(flat_encoded, w_value, preferred_element_type=jnp.float32).astype(jnp.bfloat16)

time: 298 us -> 368 us (1.23)
  waiting for transfers between devices: 116 us -> 178 us
  starting transfers between devices: 41.3 us -> 47.9 us
  local copies, waits for them, and re-layouts: 31.8 us -> 36.3 us
    all_to_all x0 -> x1, waiting for transfers between devices: none -> 108 us  [shards(): formed = lax.all_to_all(passed, 'tensor', 0, 0)]
    all_gather x1 -> x0, waiting for transfers between devices: 46.8 us -> none  [shards(): encoded = lax.all_gather(mine, 'tensor', axis=1, tiled=True)]
    all_to_all x0 -> x1, starting transfers between devices: none -> 6.87 us  [shards(): formed = lax.all_to_all(passed, 'tensor', 0, 0)]
  transfers between devices with their start and end apart: 12 -> 12, of which waited for: 6 -> 6; matrix products, arithmetic and copies ran while one was open for 17% -> 14% of each run, Pallas kernels for 0% -> 0%
where the time goes in v1:
time: 368 us; the launch traced here: 367 us
  waiting for transfers between devices  178 us (48%)
  starting transfers between devices  47.9 us (13%)
  blocking collectives  42 us (11%)
  matrix products  39.8 us (11%)
  local copies, waits for them, and re-layouts  36.3 us (10%)
  between operations  13.8 us (4%)
  other arithmetic  9.36 us (3%)
    all_to_all x1, waiting for transfers between devices, shards(): formed = lax.all_to_all(passed, 'tensor', 0, 0)  108 us
    all_to_all x1, starting transfers between devices, shards(): lax.all_to_all(requests, 'dp', split_axis=0, concat_axis=0, tiled=True)  27 us
    all_to_all x1, waiting for transfers between devices, shards(): lax.all_to_all(served, 'dp', split_axis=0, concat_axis=0, tiled=True)  25.4 us
    all_gather x1, blocking collectives, shards(): up_all = lax.all_gather(lax.all_gather(up_piece, 'tensor'), 'dp')  23.3 us
    all_gather x1, waiting for transfers between devices, shards(): down_all = lax.all_gather(lax.all_gather(down_piece, 'tensor'), 'dp')  20.9 us
    all_gather x1, blocking collectives, shards(): down_all = lax.all_gather(lax.all_gather(down_piece, 'tensor'), 'dp')  18.7 us
    ppermute x3, waiting for transfers between devices, ring_hops(): going_left = lax.ppermute(going_left, 'tensor', to_left)  12.4 us
    dot_general x8, matrix products, ring_query(): term = jnp.dot(got[offset], rows, preferred_element_type=jnp.float32)  11.3 us
  transfers between devices with their start and end apart: 12, of which 6 were waited for; matrix products, arithmetic and copies ran while one was open for 14% of the time, Pallas kernels for 0%

profile of v1, /device:TPU:1, one launch (start us, length us, event | category | flops | bytes accessed | tf_op | source)
XLA Modules:
  0.0 367.0 jit_solution(7654930567812031334)
XLA Ops:
  6.5 1.1 constant_dynamic-slice_fusion
  7.8 23.3 %all-gather.4 = bf16[8,28,448]{2,1,0:T(8,128)(2,1)S(1)} all-gather(bf16[1,28,448]{2,1,0:T(8,128)(2,1)S(1)} %bitcast.70), channel_id=2, replica_groups=mesh['dp'=32,'tensor'=8] {'tensor'}, dimensions={0}, use_global_device_ids=true | all-gather | bytes 225792 | tf_op jit(solution)/shard_map/all_gather | solution.py:94
  31.1 0.8 copy.95
  32.0 0.8 dynamic-slice_bitcast_fusion
  32.8 18.7 %all-gather.5 = bf16[8,14,896]{2,1,0:T(8,128)(2,1)S(1)} all-gather(bf16[1,14,896]{2,1,0:T(8,128)(2,1)S(1)} %dynamic-slice_bitcast_fusion), channel_id=4, replica_groups=mesh['dp'=32,'tensor'=8] {'tensor'}, dimensions={0}, use_global_device_ids=true | all-gather | bytes 225792 | tf_op jit(solution)/shard_map/all_gather | solution.py:95
  51.5 0.7 copy.99
  52.2 1.3 slice.6
  53.5 0.7 collective-permute-start
  54.2 2.1 collective-permute-start.1
  56.3 9.1 %collective-permute-done = bf16[705,512]{1,0:T(8,128)(2,1)S(1)} collective-permute-done((bf16[705,512]{1,0:T(8,128)(2,1)S(1)}, bf16[705,512]{1,0:T(8,128)(2,1)S(1)}, u32[]{:S(2)}, u32[]{:S(2)}) %collective-permute-start) | collective-permute-done | bytes 721952 | tf_op jit(solution)/shard_map/ppermute | solution.py:45
  66.0 0.7 all_to_all.14
  66.7 27.0 %all-to-all-start = ((s32[32,1,2]{2,1,0:T(1,128)}), s32[32,1,2]{2,1,0:T(1,128)S(1)}, u32[]{:S(2)}, u32[]{:S(2)}) async-start(s32[32,1,2]{2,1,0:T(1,128)} %bitcast.11), calls=%async_computation | async-start | bytes 32768 | tf_op jit(solution)/shard_map/all_to_all | solution.py:120
  93.8 1.2 fusion.37
  95.0 3.0 collective-permute-start.3
  98.0 1.2 fusion.38
  99.2 1.5 all-to-all-done
  101.0 12.4 %collective-permute-done.3 = bf16[705,512]{1,0:T(8,128)(2,1)} collective-permute-done((bf16[705,512]{1,0:T(8,128)(2,1)S(1)}, bf16[705,512]{1,0:T(8,128)(2,1)}, u32[]{:S(2)}, u32[]{:S(2)}) %collective-permute-start.3) | collective-permute-done | bytes 721952 | tf_op jit(solution)/shard_map/ppermute | solution.py:48
  113.4 5.3 %reshape.244 = bf16[256,32,28]{2,1,0:T(8,128)(2,1)S(1)} reshape(bf16[16,16,896]{2,1,0:T(8,128)(2,1)S(1)} %fusion.38) | data formatting | bytes 917504 | tf_op jit(solution)/shard_map/reshape | solution.py:112
  118.8 3.0 copy.96
  121.7 3.5 collective-permute-start.5
  125.3 8.6 %fusion.11 = bf16[256,8,448]{0,2,1:T(8,128)(2,1)S(1)} fusion(bf16[32,8,28,448]{3,1,0,2:T(8,128)(2,1)} %bitcast.71, bf16[256,32,28]{0,1,2:T(8,128)(2,1)} %copy.96), kind=kOutput, calls=%fused_computation.19 | convolution fusion | flops 1652424704 | bytes 8716288 | tf_op jit(solution)/shard_map/ncr,cgrh->ngh/dot_general | solution.py:113
  133.9 1.0 copy.98
  134.9 20.9 %all-gather.11.cloned.1.call-done = bf16[256,14,896]{2,0,1:T(8,128)(2,1)} async-done(((bf16[8,14,896]{2,0,1:T(8,128)(2,1)}), bf16[256,14,896]{2,0,1:T(8,128)(2,1)}) %all-gather.11.cloned.1.call-update) | async-done | bytes 6422544 | tf_op jit(solution)/shard_map/all_gather | solution.py:95
  155.8 6.7 %convert_reduce_fusion = f32[256,896]{1,0:T(8,128)S(1)} fusion(bf16[32,8,14,896]{3,1,0,2:T(8,128)(2,1)} %bitcast.72, bf16[256,8,32,14]{0,1,3,2:T(8,128)(2,1)S(1)} %bitcast.66), kind=kOutput, calls=%fused_computation.5 | convolution fusion | flops 1649442816 | bytes 9175040 | tf_op jit(solution)/shard_map/ngcr,cgre->gne/dot_general | solution.py:116
  162.5 1.1 fusion.36
  163.6 2.0 gather_fusion
  165.7 4.7 %all-to-all-start.1 = ((bf16[32,2,16,896]{3,2,1,0:T(8,128)(2,1)}), bf16[32,2,16,896]{3,2,1,0:T(8,128)(2,1)S(1)}, u32[]{:S(2)}, u32[]{:S(2)}) async-start(bf16[32,2,16,896]{3,2,1,0:T(8,128)(2,1)} %bitcast.13), calls=%async_computation.1 | async-start | bytes 3670016 | tf_op jit(solution)/shard_map/all_to_all | solution.py:122
  170.5 25.4 %all-to-all-done.1 = bf16[32,2,16,896]{3,2,1,0:T(8,128)(2,1)S(1)} async-done(((bf16[32,2,16,896]{3,2,1,0:T(8,128)(2,1)}), bf16[32,2,16,896]{3,2,1,0:T(8,128)(2,1)S(1)}, u32[]{:S(2)}, u32[]{:S(2)}) %all-to-all-start.1) | async-done | bytes 1835040 | tf_op jit(solution)/shard_map/all_to_all | solution.py:122
  196.6 2.9 stack.2
  199.4 6.9 %all-to-all-start.2 = ((bf16[8,24,16,896]{3,2,1,0:T(8,128)(2,1)}), bf16[8,24,16,896]{3,2,1,0:T(8,128)(2,1)}, u32[]{:S(2)}, u32[]{:S(2)}) async-start(bf16[8,24,16,896]{3,2,1,0:T(8,128)(2,1)} %stack.2), calls=%async_computation.2 | async-start | bytes 11010048 | tf_op jit(solution)/shard_map/all_to_all | solution.py:130
  206.3 1.3 copy.117
  207.6 1.7 fusion.50
  211.1 1.7 fusion.42
  212.8 1.7 convolution_add_fusion.2
  214.5 1.7 fusion.44
  216.2 1.7 convolution_add_fusion.1
  217.9 1.7 fusion.27
  219.6 1.7 reshape.251
  221.4 0.8 multiply_reduce_fusion.1
  222.9 108.4 %all-to-all-done.2 = bf16[8,24,16,896]{3,2,1,0:T(8,128)(2,1)} async-done(((bf16[8,24,16,896]{3,2,1,0:T(8,128)(2,1)}), bf16[8,24,16,896]{3,2,1,0:T(8,128)(2,1)}, u32[]{:S(2)}, u32[]{:S(2)}) %all-to-all-start.2) | async-done | bytes 5505056 | tf_op jit(solution)/shard_map/all_to_all | solution.py:130
  331.3 3.4 copy.107
  334.8 5.6 %multiply_reduce_fusion = (f32[3072,4]{0,1:T(4,128)S(1)}, f32[3072,4,128]{2,0,1:T(8,128)}) fusion(bf16[3072,896,1]{1,0,2:T(8,128)(2,1)S(1)} %bitcast.60, bf16[4,128,896]{2,1,0:T(8,128)(2,1)S(1)} %bitcast.68), kind=kOutput, calls=%fused_computation.9 | convolution fusion | flops 2821705728 | bytes 12763136 | tf_op jit(solution)/shard_map/dot_general | solution.py:133
  340.4 4.8 %convolution_convert_fusion = bf16[3072,512]{1,0:T(8,128)(2,1)} fusion(bf16[3072,896]{1,0:T(8,128)(2,1)S(1)} %bitcast.61, bf16[896,512]{1,0:T(8,128)(2,1)S(1)} %copy-done), kind=kOutput, calls=%fused_computation.11 | convolution fusion | flops 2820145152 | bytes 9568256 | tf_op jit(solution)/shard_map/dot_general | solution.py:134
  345.2 5.5 %reshape_reshape.7 = bf16[12,256,4,128]{3,2,1,0:T(4,128)(2,1)} reshape(bf16[3072,512]{1,0:T(8,128)(2,1)} %convolution_convert_fusion) | data formatting | bytes 6291456 | tf_op jit(solution)/shard_map/reshape;reshape | solution.py:26
  350.7 4.4 %multiply_convert_fusion = bf16[3072,4,128]{2,0,1:T(8,128)(2,1)S(1)} fusion(f32[3072,4,128]{2,0,1:T(8,128)} %get-tuple-element.12, f32[3072,4]{0,1:T(4,128)S(1)} %add_rsqrt_fusion), kind=kLoop, calls=%fused_computation.8 | loop fusion | flops 3145728 | bytes 9486336 | tf_op jit(solution)/shard_map/convert_element_type | solution.py:18
  355.2 1.3 fusion.16
  357.1 1.2 fusion.32
  359.1 1.1 concatenate.7
  (66 shorter events, 5.6 us)
Async XLA Ops:
  6.5 333.9 %copy-start = (bf16[896,512]{1,0:T(8,128)(2,1)S(1)}, bf16[896,512]{1,0:T(8,128)(2,1)}, u32[]{:S(2)}) copy-start(bf16[896,512]{1,0:T(8,128)(2,1)} %param.15) | copy-start | bytes 2752516
  6.5 58.9 %copy-start.12 = (s32[12,2]{0,1:T(2,128)S(1)}, s32[12,2]{0,1:T(2,128)}, u32[]{:S(2)}) copy-start(s32[12,2]{0,1:T(2,128)} %param.9) | copy-start | bytes 292
  6.5 118.7 %all-gather.9.cloned.1.call-start = ((), (), s32[]{:S(2)}) async-start(), calls=%async_computation.3 | async-start | bytes 7569408 | tf_op jit(solution)/shard_map/all_gather | solution.py:94
  31.9 123.9 %all-gather.11.cloned.1.call-start = ((), (), s32[]{:S(2)}) async-start(), calls=%async_computation.4 | async-start | bytes 6623232 | tf_op jit(solution)/shard_map/all_gather | solution.py:95
  53.5 11.9 %collective-permute-start = (bf16[705,512]{1,0:T(8,128)(2,1)S(1)}, bf16[705,512]{1,0:T(8,128)(2,1)S(1)}, u32[]{:S(2)}, u32[]{:S(2)}) collective-permute-start(bf16[705,512]{1,0:T(8,128)(2,1)S(1)} %slice.6), channel_id=1, source_target_pairs={{0,1},{1,2},{2,3},{3,4},{4,5},{5,6},{6,7},{7,0},{8,9},{9,10},{10,1... | collective-permute-start | bytes 2165768 | tf_op jit(solution)/shard_map/ppermute | solution.py:45
  54.2 40.7 %collective-permute-start.1 = (bf16[705,512]{1,0:T(8,128)(2,1)S(1)}, bf16[705,512]{1,0:T(8,128)(2,1)S(1)}, u32[]{:S(2)}, u32[]{:S(2)}) collective-permute-start(bf16[705,512]{1,0:T(8,128)(2,1)S(1)} %slice.6), channel_id=1, source_target_pairs={{0,7},{1,0},{2,1},{3,2},{4,3},{5,4},{6,5},{7,6},{8,15},{9,8},{10,9... | collective-permute-start | bytes 2165768 | tf_op jit(solution)/shard_map/ppermute | solution.py:48
  65.4 35.6 %copy-start.7 = (bf16[705,512]{1,0:T(8,128)(2,1)}, bf16[705,512]{1,0:T(8,128)(2,1)S(1)}, u32[]{:S(2)}) copy-start(bf16[705,512]{1,0:T(8,128)(2,1)S(1)} %collective-permute-done) | copy-start | bytes 2165764
  65.4 32.6 %collective-permute-start.2 = (bf16[705,512]{1,0:T(8,128)(2,1)S(1)}, bf16[705,512]{1,0:T(8,128)(2,1)}, u32[]{:S(2)}, u32[]{:S(2)}) collective-permute-start(bf16[705,512]{1,0:T(8,128)(2,1)S(1)} %collective-permute-done), channel_id=1, source_target_pairs={{0,1},{1,2},{2,3},{3,4},{4,5},{5,6},{6,7},{7,0},{8,9},{9,10},{10,1... | collective-permute-start | bytes 2165768 | tf_op jit(solution)/shard_map/ppermute | solution.py:45
  66.7 34.0 %all-to-all-start = ((s32[32,1,2]{2,1,0:T(1,128)}), s32[32,1,2]{2,1,0:T(1,128)S(1)}, u32[]{:S(2)}, u32[]{:S(2)}) async-start(s32[32,1,2]{2,1,0:T(1,128)} %bitcast.11), calls=%async_computation | async-start | bytes 32768 | tf_op jit(solution)/shard_map/all_to_all | solution.py:120
  95.0 6.1 %copy-start.9 = (bf16[705,512]{1,0:T(8,128)(2,1)}, bf16[705,512]{1,0:T(8,128)(2,1)S(1)}, u32[]{:S(2)}) copy-start(bf16[705,512]{1,0:T(8,128)(2,1)S(1)} %collective-permute-done.1) | copy-start | bytes 2165764
  95.0 18.5 %collective-permute-start.3 = (bf16[705,512]{1,0:T(8,128)(2,1)S(1)}, bf16[705,512]{1,0:T(8,128)(2,1)}, u32[]{:S(2)}, u32[]{:S(2)}) collective-permute-start(bf16[705,512]{1,0:T(8,128)(2,1)S(1)} %collective-permute-done.1), channel_id=1, source_target_pairs={{0,7},{1,0},{2,1},{3,2},{4,3},{5,4},{6,5},{7,6},{8,15},{9,8},{10,9... | collective-permute-start | bytes 2165768 | tf_op jit(solution)/shard_map/ppermute | solution.py:48
  98.0 27.3 %collective-permute-start.4 = (bf16[705,512]{1,0:T(8,128)(2,1)}, bf16[705,512]{1,0:T(8,128)(2,1)}, u32[]{:S(2)}, u32[]{:S(2)}) collective-permute-start(bf16[705,512]{1,0:T(8,128)(2,1)} %collective-permute-done.2), channel_id=1, source_target_pairs={{0,1},{1,2},{2,3},{3,4},{4,5},{5,6},{6,7},{7,0},{8,9},{9,10},{10,1... | collective-permute-start | bytes 2165768 | tf_op jit(solution)/shard_map/ppermute | solution.py:45
  121.7 43.9 %collective-permute-start.5 = (bf16[705,512]{1,0:T(8,128)(2,1)}, bf16[705,512]{1,0:T(8,128)(2,1)}, u32[]{:S(2)}, u32[]{:S(2)}) collective-permute-start(bf16[705,512]{1,0:T(8,128)(2,1)} %collective-permute-done.3), channel_id=1, source_target_pairs={{0,7},{1,0},{2,1},{3,2},{4,3},{5,4},{6,5},{7,6},{8,15},{9,8},{10,9... | collective-permute-start | bytes 2165768 | tf_op jit(solution)/shard_map/ppermute | solution.py:48
  125.3 40.4 %collective-permute-start.6 = (bf16[705,512]{1,0:T(8,128)(2,1)}, bf16[705,512]{1,0:T(8,128)(2,1)S(1)}, u32[]{:S(2)}, u32[]{:S(2)}) collective-permute-start(bf16[705,512]{1,0:T(8,128)(2,1)} %collective-permute-done.4), channel_id=1, source_target_pairs={{0,1},{1,2},{2,3},{3,4},{4,5},{5,6},{6,7},{7,0},{8,9},{9,10},{10,1... | collective-permute-start | bytes 2165768 | tf_op jit(solution)/shard_map/ppermute | solution.py:45
  165.7 30.2 %copy-start.5 = (bf16[705,512]{1,0:T(8,128)(2,1)}, bf16[705,512]{1,0:T(8,128)(2,1)S(1)}, u32[]{:S(2)}) copy-start(bf16[705,512]{1,0:T(8,128)(2,1)S(1)} %collective-permute-done.6) | copy-start | bytes 2165764
  165.7 30.2 %all-to-all-start.1 = ((bf16[32,2,16,896]{3,2,1,0:T(8,128)(2,1)}), bf16[32,2,16,896]{3,2,1,0:T(8,128)(2,1)S(1)}, u32[]{:S(2)}, u32[]{:S(2)}) async-start(bf16[32,2,16,896]{3,2,1,0:T(8,128)(2,1)} %bitcast.13), calls=%async_computation.1 | async-start | bytes 3670016 | tf_op jit(solution)/shard_map/all_to_all | solution.py:122
  199.4 6.9 %copy-start.3 = (bf16[896,512]{1,0:T(8,128)(2,1)S(1)}, bf16[896,512]{1,0:T(8,128)(2,1)}, u32[]{:S(2)}) copy-start(bf16[896,512]{1,0:T(8,128)(2,1)} %param.14) | copy-start | bytes 2752516
  199.4 8.2 %copy-start.11 = (bf16[768,512]{1,0:T(8,128)(2,1)S(1)}, bf16[768,512]{1,0:T(8,128)(2,1)}, u32[]{:S(2)}) copy-start(bf16[768,512]{1,0:T(8,128)(2,1)} %param.8) | copy-start | bytes 2359300
  199.4 131.9 %all-to-all-start.2 = ((bf16[8,24,16,896]{3,2,1,0:T(8,128)(2,1)}), bf16[8,24,16,896]{3,2,1,0:T(8,128)(2,1)}, u32[]{:S(2)}, u32[]{:S(2)}) async-start(bf16[8,24,16,896]{3,2,1,0:T(8,128)(2,1)} %stack.2), calls=%async_computation.2 | async-start | bytes 11010048 | tf_op jit(solution)/shard_map/all_to_all | solution.py:130
  206.3 3.1 copy-start.8
  207.6 2.3 copy-start.1
  207.6 2.9 copy-start.10
  214.5 3.4 copy-start.6
  331.3 3.4 copy-start.4
  355.2 1.9 copy-start.2
Sparse Core Ops, SparseCore 0:
  32.0 66.9 all-gather.8
  101.6 54.1 all-gather.10
